TPU v7x, 32 devices: a whole 2x2x4 slice. The times are simulated.
32 devices in a mesh: exp: 4 (over z), row: 4 (over y, core), col: 2 (over x).
Axes of the slice: x: 2, y: 2, z: 4, core: 2. Of those that a mesh axis runs over, the one named last changes fastest.
Arguments:
- exposures: float32 [64, 128, 1024], P('exp', 'row', 'col'), may hold values from -6 to 6
- bad_pixels: int32 [64, 128, 1024], P('exp', 'row', 'col'), may hold values 0 or 1
- offsets: int32 [64, 2], P('exp'), may hold values from -8 to 8, as said below
- warp_index: int32 [64, 2], P('exp'), may hold values from 0 to 15
- blur_index: int32 [64], P('exp'), may hold values from 0 to 7
Outputs:
- residual: float32 [64, 128, 1024], P('exp', 'row', 'col')
- median_sky: float32 [128, 1024], P('row', 'col')
Inputs may be any that keep to these rules, and one draw needn't show every extreme that they name: `offsets`: in each component some exposure has the offset -8 and some has 8.
All inputs are finite; a program needn't handle non-finite values. No bound on the sum of `bad_pixels` on one device may be relied on, other than what follows from the above.
Results may differ from a plain program's by a relative error of at most 0.0003.
Values sent between devices are 32-bit elements; how exact they have to be, the bound alone decides.
No kernel may reach another device: no remote copies, remote signals or barrier semaphores. Data moves between devices by JAX's collectives and lax.ppermute only.
A program may use at most 64 MiB of HBM per device.

v0:
```python
import jax
import jax.numpy as jnp
from jax import lax
from jax.sharding import PartitionSpec as P

NFRAC = 16
NPSF = 8
PSF_RADIUS = 4
PASSES = 16
HALO = 11
sentinel = 1000000.0
half_sentinel = 500000.0
pivot_span = 16.0


def _row_halo(block, dim, width):
    count = lax.axis_size("row")
    forward = [(i, i + 1) for i in range(count - 1)]
    backward = [(target, source) for source, target in forward]
    size = block.shape[dim]
    low = lax.ppermute(lax.slice_in_dim(block, size - width, None, axis=dim), "row", forward)
    high = lax.ppermute(lax.slice_in_dim(block, 0, width, axis=dim), "row", backward)
    return jnp.concatenate([low, block, high], axis=dim)


def _col_halo(block, dim, width):
    count = lax.axis_size("col")
    size = block.shape[dim]
    right_edge = lax.slice_in_dim(block, size - width, None, axis=dim)
    left_edge = lax.slice_in_dim(block, 0, width, axis=dim)
    if count != 2:
        forward = [(i, i + 1) for i in range(count - 1)]
        backward = [(target, source) for source, target in forward]
        low = lax.ppermute(right_edge, "col", forward)
        high = lax.ppermute(left_edge, "col", backward)
        return jnp.concatenate([low, block, high], axis=dim)
    first = lax.axis_index("col") == 0
    outgoing = jnp.moveaxis(jnp.where(first, right_edge, left_edge), dim, 0)
    packed_shape = outgoing.shape
    packed = outgoing.reshape(width, -1)
    arrived = lax.ppermute(packed, "col", [(0, 1), (1, 0)])
    arrived = jnp.moveaxis(arrived.reshape(packed_shape), 0, dim)
    zeros = jnp.zeros_like(arrived)
    low = jnp.where(first, zeros, arrived)
    high = jnp.where(first, arrived, zeros)
    return jnp.concatenate([low, block, high], axis=dim)


def extended(block, row_dim, col_dim, width):
    return _col_halo(_row_halo(block, row_dim, width), col_dim, width)


def lanczos_table():
    fraction = jnp.arange(NFRAC, dtype=jnp.float32) / NFRAC
    offset_grid = jnp.arange(-2, 4, dtype=jnp.float32)
    spread = offset_grid[None, :] - fraction[:, None]
    kernel = jnp.sinc(spread) * jnp.sinc(spread / 3.0)
    return kernel / jnp.sum(kernel, axis=1, keepdims=True)


def blur_table():
    offset_grid = jnp.arange(-PSF_RADIUS, PSF_RADIUS + 1, dtype=jnp.float32)
    widths = 0.7 + 0.2 * jnp.arange(NPSF, dtype=jnp.float32)
    kernel = jnp.exp(-0.5 * (offset_grid[None, :] / widths[:, None]) ** 2)
    return kernel / jnp.sum(kernel, axis=1, keepdims=True)


def lookup(indices, entries, kernel_table):
    chooser = (indices[:, None] == lax.broadcasted_iota(jnp.int32, (1, entries), 1)).astype(
        jnp.float32
    )
    return jnp.dot(chooser, kernel_table, precision=lax.Precision.HIGHEST)


def placed_taps(weights, shifts):
    reach = 2 * HALO + 1
    positions = lax.broadcasted_iota(jnp.int32, (1, 1, reach), 2)
    tap_slot = HALO + shifts[:, None, None] + lax.broadcasted_iota(jnp.int32, (1, 6, 1), 1) - 2
    spread = (tap_slot == positions).astype(jnp.float32)
    return jnp.sum(weights[:, :, None] * spread, axis=1)


def resample_axis(stack, coefficients, out_len, which_axis):
    out_shape = list(stack.shape)
    out_shape[which_axis] = out_len
    total = jnp.zeros(tuple(out_shape), jnp.float32)
    for position in range(2 * HALO + 1):
        window = lax.slice_in_dim(stack, position, position + out_len, 1, which_axis)
        total = total + coefficients[:, position, None, None] * window
    return total


def bisect_lower(valid_count, count_below):

    def one_pass(sweep_no, bounds):
        lower_edge, upper_edge = bounds
        middle = 0.5 * (lower_edge + upper_edge)
        enough = 2.0 * count_below(middle) >= valid_count
        return (jnp.where(enough, lower_edge, middle), jnp.where(enough, middle, upper_edge))

    initial = (
        jnp.full(valid_count.shape, -pivot_span, jnp.float32),
        jnp.full(valid_count.shape, pivot_span, jnp.float32),
    )
    return lax.fori_loop(0, PASSES, one_pass, initial)[0]


def stack_median(pixel_stack):
    valid_count = jnp.sum(pixel_stack < half_sentinel, axis=0, dtype=jnp.float32)

    def count_below(middle):
        return jnp.sum(pixel_stack <= middle[None], axis=0, dtype=jnp.float32)

    lower_edge = bisect_lower(valid_count, count_below)
    return jnp.min(jnp.where(pixel_stack > lower_edge[None], pixel_stack, sentinel), axis=0)


def body(exposures, bad_pixels, offsets, warp_index, blur_index):
    group_size, row_count, col_count = exposures.shape
    kernel_table = lanczos_table()
    coef_down = placed_taps(lookup(warp_index[:, 0], NFRAC, kernel_table), offsets[:, 0])
    coef_across = placed_taps(lookup(warp_index[:, 1], NFRAC, kernel_table), offsets[:, 1])
    padded = extended(exposures, 1, 2, HALO)
    across = resample_axis(padded, coef_down, row_count, 1)
    warped = resample_axis(across, coef_across, col_count, 2)
    flagged = jnp.where(bad_pixels == 1, sentinel, warped)
    band = stack_median(lax.all_to_all(flagged, "exp", split_axis=1, concat_axis=0, tiled=True))
    groups = lax.axis_size("exp")
    median_sky = lax.all_to_all(
        jnp.tile(band, (groups, 1)), "exp", split_axis=0, concat_axis=0, tiled=True
    )
    bordered = extended(median_sky, 0, 1, PSF_RADIUS)
    blur = blur_table()
    taps = 2 * PSF_RADIUS + 1
    blurred_rows = jnp.zeros((NPSF, row_count, col_count + 2 * PSF_RADIUS), jnp.float32)
    for tap_no in range(taps):
        blurred_rows = (
            blurred_rows
            + blur[:, tap_no, None, None] * bordered[None, tap_no : tap_no + row_count, :]
        )
    smoothed = jnp.zeros((NPSF, row_count, col_count), jnp.float32)
    for tap_no in range(taps):
        smoothed = (
            smoothed + blur[:, tap_no, None, None] * blurred_rows[:, :, tap_no : tap_no + col_count]
        )
    chooser = (blur_index[:, None] == lax.broadcasted_iota(jnp.int32, (1, NPSF), 1)).astype(
        jnp.float32
    )
    sky_model = jnp.zeros((group_size, row_count, col_count), jnp.float32)
    for kernel_no in range(NPSF):
        sky_model = sky_model + chooser[:, kernel_no, None, None] * smoothed[kernel_no][None]
    residual = jnp.where(bad_pixels == 1, 0.0, warped - sky_model)
    return (residual, median_sky)


def solution(mesh):
    return jax.shard_map(
        body,
        mesh=mesh,
        in_specs=(
            P("exp", "row", "col"),
            P("exp", "row", "col"),
            P("exp", None),
            P("exp", None),
            P("exp"),
        ),
        out_specs=(P("exp", "row", "col"), P("row", "col")),
        check_vma=False,
    )
```

profile of v0, /device:TPU:0, one launch (start us, length us, event | category | flops | bytes accessed | tf_op | source)
XLA Modules:
  0.0 90.9 jit_solution(72379477720639308)
XLA Ops:
  0.6 1.3 %fusion.134 = (f32[16,11,512]{2,1,0:T(8,128)S(1)}, f32[16,11,512]{2,1,0:T(8,128)S(1)}) fusion(f32[16,32,512]{2,1,0:T(8,128)} %param.8), kind=kLoop, calls=%fused_computation.315 | loop fusion | bytes 1441792 | tf_op jit(solution)/shard_map/slice | solution.py:22
  2.0 0.2 copy.47
  2.2 3.3 %collective-permute-start = (f32[16,11,512]{2,0,1:T(8,128)S(1)}, f32[16,11,512]{2,0,1:T(8,128)}, u32[]{:S(2)}, u32[]{:S(2)}) collective-permute-start(f32[16,11,512]{2,0,1:T(8,128)S(1)} %copy.47), channel_id=1, source_target_pairs={{0,2},{2,4},{4,6},{1,3},{3,5},{5,7},{8,10},{10,12},{12,14},{9,11},... | collective-permute-start | bytes 1081352 | tf_op jit(solution)/shard_map/ppermute | solution.py:21
  5.5 0.2 copy.48
  5.7 1.3 %collective-permute-start.1 = (f32[16,11,512]{2,0,1:T(8,128)S(1)}, f32[16,11,512]{2,0,1:T(8,128)S(1)}, u32[]{:S(2)}, u32[]{:S(2)}) collective-permute-start(f32[16,11,512]{2,0,1:T(8,128)S(1)} %copy.48), channel_id=1, source_target_pairs={{2,0},{4,2},{6,4},{3,1},{5,3},{7,5},{10,8},{12,10},{14,12},{11,9},... | collective-permute-start | bytes 1081352 | tf_op jit(solution)/shard_map/ppermute | solution.py:22
  7.1 0.1 fusion.108
  7.2 0.2 fusion.67
  7.4 0.2 fusion.66
  7.6 0.1 select_reduce_fusion
  7.7 0.8 slice_reduce_fusion.43
  8.5 1.1 %slice_reduce_fusion.44 = (f32[16]{0:T(128)}, f32[16]{0:T(128)}, f32[16]{0:T(128)}, f32[16]{0:T(128)}, f32[16]{0:T(128)}, /*index=5*/f32[16]{0:T(128)}, f32[16]{...) fusion(f32[16,23]{1,0:T(8,128)S(1)} %select_reduce_fusion), kind=kLoop, calls=%fused_computation.204 | loop fusion | bytes 2432 | tf_op jit(solution)/shard_map/slice | solution.py:89
  9.7 1.1 %slice_reduce_fusion.45 = (f32[16]{0:T(128)S(1)}, f32[16]{0:T(128)S(1)}, f32[16]{0:T(128)}, f32[16]{0:T(128)}, f32[16]{0:T(128)}, /*index=5*/f32[16]{0:T(128)}, ...) fusion(f32[16,23]{1,0:T(8,128)S(1)} %select_reduce_fusion.1), kind=kLoop, calls=%fused_computation.205 | loop fusion | bytes 2432 | tf_op jit(solution)/shard_map/slice | solution.py:89
  10.7 1.0 %constant_dynamic-update-slice_fusion.2 = f32[16,54,512]{2,0,1:T(8,128)S(1)} fusion(f32[16,11,512]{2,0,1:T(8,128)} %collective-permute-done), kind=kLoop, calls=%fused_computation.208 | loop fusion | bytes 720896
  11.8 0.6 constant_dynamic-update-slice_fusion.1
  12.4 0.2 fusion.53
  12.6 0.3 copy.40
  12.9 0.1 reshape.187
  13.0 2.4 %collective-permute-start.2 = (f32[11,864]{1,0:T(8,128)S(1)}, f32[11,864]{1,0:T(8,128)S(1)}, u32[]{:S(2)}, u32[]{:S(2)}) collective-permute-start(f32[11,864]{1,0:T(8,128)S(1)} %reshape.187), channel_id=1, source_target_pairs={{0,1},{1,0},{2,3},{3,2},{4,5},{5,4},{6,7},{7,6},{8,9},{9,8},{10,11... | collective-permute-start | bytes 114056 | tf_op jit(solution)/shard_map/ppermute | solution.py:41
  15.4 0.2 slice_reduce_fusion.21
  15.6 1.9 %collective-permute-done.2 = f32[11,864]{1,0:T(8,128)S(1)} collective-permute-done((f32[11,864]{1,0:T(8,128)S(1)}, f32[11,864]{1,0:T(8,128)S(1)}, u32[]{:S(2)}, u32[]{:S(2)}) %collective-permute-start.2) | collective-permute-done | bytes 38048 | tf_op jit(solution)/shard_map/ppermute | solution.py:41
  17.5 0.1 select_n.97
  17.6 0.3 copy.42
  18.0 0.1 select_n.94
  18.1 0.3 copy.41
  18.6 0.7 pad_maximum_fusion
  19.8 3.9 %fusion = f32[16,32,534]{2,0,1:T(8,128)S(1)} fusion(f32[16,54,534]{2,0,1:T(8,128)S(1)} %pad_maximum_fusion, f32[16]{0:T(128)S(1)} %copy-done.24, f32[16]{0:T(128)S(1)} %copy-done.25, f32[16]{0:T(128)S(1)} %copy-done.26, f32[16]{0:T(128)S(1)} %copy-done.27, f32[16]{0:T(128)S(1)} %copy-done.28, f32[16]{0:T(128)S(1)} %copy-done.29, f32[16]{0:T(128)S(1)} %copy-done.30, ...), kind=kLoop, calls=%fused_computation.8 | loop fusion | flops 12303360 | bytes 26248640 | tf_op jit(solution)/shard_map/add | solution.py:89
  23.8 7.0 %broadcast_select_fusion = (f32[16,32,512]{2,0,1:T(8,128)}, f32[16,32,512]{2,0,1:T(8,128)S(1)}, pred[16,32,512]{2,0,1:T(8,128)(4,1)S(1)}) fusion(f32[16,32,534]{2,0,1:T(8,128)S(1)} %fusion, f32[16]{0:T(128)S(1)} %get-tuple-element.56, f32[16]{0:T(128)S(1)} %copy-done.2, f32[16]{0:T(128)S(1)} %copy-done.3, f32[16]{0:T(128)S(1)} %copy-done.4, ...), kind=kLoop, calls=%fused_computation.119 | loop fusion | flops 12320768 | bytes 27526592 | tf_op jit(solution)/shard_map/jit(_where)/select_n | solution.py:126
  30.8 5.4 %all-to-all-start = ((f32[16,32,512]{2,0,1:T(8,128)}), f32[16,32,512]{2,0,1:T(8,128)S(1)}, u32[]{:S(2)}, u32[]{:S(2)}) async-start(f32[16,32,512]{2,0,1:T(8,128)} %get-tuple-element.113), calls=%async_computation | async-start | bytes 2097152 | tf_op jit(solution)/shard_map/all_to_all | solution.py:127
  36.2 0.1 fusion.72
  36.4 26.2 %all-to-all-done = f32[16,32,512]{2,0,1:T(8,128)S(1)} async-done(((f32[16,32,512]{2,0,1:T(8,128)}), f32[16,32,512]{2,0,1:T(8,128)S(1)}, u32[]{:S(2)}, u32[]{:S(2)}) %all-to-all-start) | async-done | bytes 1048608 | tf_op jit(solution)/shard_map/all_to_all | solution.py:127
  62.6 0.6 copy.43
  63.2 0.1 convert_reduce_fusion.1
  63.4 3.6 %while.13 = (s32[]{:T(128)}, f32[8,512]{1,0:T(8,128)S(1)}, f32[8,512]{1,0:T(8,128)S(1)}, f32[64,8,512]{2,1,0:T(8,128)S(1)}, f32[8,512]{1,0:T(8,128)S(1)}, /*index=5*/s32[]{:T(128)}, s32[]{:T(128)}) while((s32[]{:T(128)}, f32[8,512]{1,0:T(8,128)S(1)}, f32[8,512]{1,0:T(8,128)S(1)}, f32[64,8,512]{2,1,0:T(8,128)S(1)}, ...), condition=%wide.region_7.9_spmd.clone, body=%wide.region_5.8_spmd.clone.sunk | while | flops 1110019 | bytes 1302625 | solution.py:105
  63.4 0.1 convert_reduce_fusion.3
  63.6 0.1 convert_reduce_fusion.3
  63.9 0.1 convert_reduce_fusion.3
  64.1 0.1 convert_reduce_fusion.3
  64.3 0.1 convert_reduce_fusion.3
  64.5 0.1 convert_reduce_fusion.3
  64.8 0.1 convert_reduce_fusion.3
  65.0 0.1 convert_reduce_fusion.3
  65.2 0.1 convert_reduce_fusion.3
  65.4 0.1 convert_reduce_fusion.3
  65.7 0.1 convert_reduce_fusion.3
  65.9 0.1 convert_reduce_fusion.3
  66.1 0.1 convert_reduce_fusion.3
  66.4 0.1 convert_reduce_fusion.3
  66.6 0.1 convert_reduce_fusion.3
  66.8 0.1 convert_reduce_fusion.3
  67.0 0.2 fusion.22
  67.2 0.6 tile.2
  67.8 3.3 %all-to-all-start.1 = ((f32[4,8,512]{2,1,0:T(8,128)}), f32[4,8,512]{2,1,0:T(8,128)S(1)}, u32[]{:S(2)}, u32[]{:S(2)}) async-start(f32[4,8,512]{2,1,0:T(8,128)} %tile.2), calls=%async_computation.1 | async-start | bytes 131072 | tf_op jit(solution)/shard_map/all_to_all | solution.py:129
  71.1 5.8 %all-to-all-done.1 = f32[4,8,512]{2,1,0:T(8,128)S(1)} async-done(((f32[4,8,512]{2,1,0:T(8,128)}), f32[4,8,512]{2,1,0:T(8,128)S(1)}, u32[]{:S(2)}, u32[]{:S(2)}) %all-to-all-start.1) | async-done | bytes 65568 | tf_op jit(solution)/shard_map/all_to_all | solution.py:129
  76.9 1.3 %collective-permute-start.4 = (f32[4,512]{1,0:T(4,128)S(1)}, f32[4,512]{1,0:T(4,128)S(1)}, u32[]{:S(2)}, u32[]{:S(2)}) collective-permute-start(f32[4,512]{1,0:T(4,128)S(1)} %get-tuple-element.136), channel_id=1, source_target_pairs={{2,0},{4,2},{6,4},{3,1},{5,3},{7,5},{10,8},{12,10},{14,12},{11,9},... | collective-permute-start | bytes 24584 | tf_op jit(solution)/shard_map/ppermute | solution.py:22
  78.2 3.2 %collective-permute-start.3 = (f32[4,512]{1,0:T(4,128)S(1)}, f32[4,512]{1,0:T(4,128)S(1)}, u32[]{:S(2)}, u32[]{:S(2)}) collective-permute-start(f32[4,512]{1,0:T(4,128)S(1)} %get-tuple-element.135), channel_id=1, source_target_pairs={{0,2},{2,4},{4,6},{1,3},{3,5},{5,7},{8,10},{10,12},{12,14},{9,11},... | collective-permute-start | bytes 24584 | tf_op jit(solution)/shard_map/ppermute | solution.py:21
  81.5 0.6 collective-permute-done.3
  82.1 1.5 %collective-permute-start.5 = (f32[4,40]{0,1:T(8,128)S(1)}, f32[4,40]{0,1:T(8,128)S(1)}, u32[]{:S(2)}, u32[]{:S(2)}) collective-permute-start(f32[4,40]{0,1:T(8,128)S(1)} %fusion.55), channel_id=1, source_target_pairs={{0,1},{1,0},{2,3},{3,2},{4,5},{5,4},{6,7},{7,6},{8,9},{9,8},{10,11... | collective-permute-start | bytes 1928 | tf_op jit(solution)/shard_map/ppermute | solution.py:41
  83.7 2.3 %collective-permute-done.5 = f32[4,40]{0,1:T(8,128)S(1)} collective-permute-done((f32[4,40]{0,1:T(8,128)S(1)}, f32[4,40]{0,1:T(8,128)S(1)}, u32[]{:S(2)}, u32[]{:S(2)}) %collective-permute-start.5) | collective-permute-done | bytes 672 | tf_op jit(solution)/shard_map/ppermute | solution.py:41
  85.9 0.1 pad_maximum_fusion.1
  86.1 0.6 multiply_add_fusion
  86.7 1.3 %fusion.45 = f32[8,32,512]{2,1,0:T(8,128)S(1)} fusion(f32[8,32,520]{2,1,0:T(8,128)S(1)} %multiply_add_fusion, f32[8]{0:T(128)S(1)} %get-tuple-element.142, f32[8]{0:T(128)S(1)} %get-tuple-element.143, f32[8]{0:T(128)S(1)} %get-tuple-element.144, f32[8]{0:T(128)S(1)} %get-tuple-element.145, f32[8]{0:T(128)S(1)} %get-tuple-element.146, ...), kind=kLoop, calls=%fused_computation.103 | loop fusion | flops 2228224 | bytes 5243168 | tf_op jit(solution)/shard_map/add | solution.py:144
  88.0 0.7 subtract_select_fusion
  88.7 1.6 %copy.44 = f32[16,32,512]{2,1,0:T(8,128)} copy(f32[16,32,512]{2,0,1:T(8,128)S(1)} %subtract_select_fusion) | data formatting | bytes 2097152
  90.3 0.6 copy.62
  (176 shorter events, 1.2 us)
Async XLA Ops:
  2.0 5.1 %copy-start.41 = (s32[16,2]{0,1:T(2,128)S(1)}, s32[16,2]{0,1:T(2,128)}, u32[]{:S(2)}) copy-start(s32[16,2]{0,1:T(2,128)} %param.11) | copy-start | bytes 388
  2.0 5.1 %copy-start.42 = (s32[16,2]{0,1:T(2,128)S(1)}, s32[16,2]{0,1:T(2,128)}, u32[]{:S(2)}) copy-start(s32[16,2]{0,1:T(2,128)} %param.10) | copy-start | bytes 388
  2.2 9.6 %copy-start = (f32[16,32,512]{2,1,0:T(8,128)S(1)}, f32[16,32,512]{2,1,0:T(8,128)}, u32[]{:S(2)}) copy-start(f32[16,32,512]{2,1,0:T(8,128)} %param.8) | copy-start | bytes 3145732
  2.2 8.5 %collective-permute-start = (f32[16,11,512]{2,0,1:T(8,128)S(1)}, f32[16,11,512]{2,0,1:T(8,128)}, u32[]{:S(2)}, u32[]{:S(2)}) collective-permute-start(f32[16,11,512]{2,0,1:T(8,128)S(1)} %copy.47), channel_id=1, source_target_pairs={{0,2},{2,4},{4,6},{1,3},{3,5},{5,7},{8,10},{10,12},{12,14},{9,11},... | collective-permute-start | bytes 1081352 | tf_op jit(solution)/shard_map/ppermute | solution.py:21
  5.7 6.7 %collective-permute-start.1 = (f32[16,11,512]{2,0,1:T(8,128)S(1)}, f32[16,11,512]{2,0,1:T(8,128)S(1)}, u32[]{:S(2)}, u32[]{:S(2)}) collective-permute-start(f32[16,11,512]{2,0,1:T(8,128)S(1)} %copy.48), channel_id=1, source_target_pairs={{2,0},{4,2},{6,4},{3,1},{5,3},{7,5},{10,8},{12,10},{14,12},{11,9},... | collective-permute-start | bytes 1081352 | tf_op jit(solution)/shard_map/ppermute | solution.py:22
  13.0 4.5 %collective-permute-start.2 = (f32[11,864]{1,0:T(8,128)S(1)}, f32[11,864]{1,0:T(8,128)S(1)}, u32[]{:S(2)}, u32[]{:S(2)}) collective-permute-start(f32[11,864]{1,0:T(8,128)S(1)} %reshape.187), channel_id=1, source_target_pairs={{0,1},{1,0},{2,3},{3,2},{4,5},{5,4},{6,7},{7,6},{8,9},{9,8},{10,11... | collective-permute-start | bytes 114056 | tf_op jit(solution)/shard_map/ppermute | solution.py:41
  18.4 1.0 %copy-start.19 = (f32[16]{0:T(128)S(1)}, f32[16]{0:T(128)}, u32[]{:S(2)}) copy-start(f32[16]{0:T(128)} %get-tuple-element.97) | copy-start | bytes 196
  18.4 1.0 %copy-start.20 = (f32[16]{0:T(128)S(1)}, f32[16]{0:T(128)}, u32[]{:S(2)}) copy-start(f32[16]{0:T(128)} %get-tuple-element.98) | copy-start | bytes 196
  18.4 1.0 %copy-start.21 = (f32[16]{0:T(128)S(1)}, f32[16]{0:T(128)}, u32[]{:S(2)}) copy-start(f32[16]{0:T(128)} %get-tuple-element.99) | copy-start | bytes 196
  18.4 1.0 %copy-start.22 = (f32[16]{0:T(128)S(1)}, f32[16]{0:T(128)}, u32[]{:S(2)}) copy-start(f32[16]{0:T(128)} %get-tuple-element.100) | copy-start | bytes 196
  18.4 1.0 %copy-start.23 = (f32[16]{0:T(128)S(1)}, f32[16]{0:T(128)}, u32[]{:S(2)}) copy-start(f32[16]{0:T(128)} %get-tuple-element.78) | copy-start | bytes 196
  18.4 1.0 %copy-start.24 = (f32[16]{0:T(128)S(1)}, f32[16]{0:T(128)}, u32[]{:S(2)}) copy-start(f32[16]{0:T(128)} %get-tuple-element.79) | copy-start | bytes 196
  18.5 1.0 %copy-start.25 = (f32[16]{0:T(128)S(1)}, f32[16]{0:T(128)}, u32[]{:S(2)}) copy-start(f32[16]{0:T(128)} %get-tuple-element.80) | copy-start | bytes 196
  18.5 1.0 %copy-start.26 = (f32[16]{0:T(128)S(1)}, f32[16]{0:T(128)}, u32[]{:S(2)}) copy-start(f32[16]{0:T(128)} %get-tuple-element.81) | copy-start | bytes 196
  18.5 1.0 %copy-start.27 = (f32[16]{0:T(128)S(1)}, f32[16]{0:T(128)}, u32[]{:S(2)}) copy-start(f32[16]{0:T(128)} %get-tuple-element.82) | copy-start | bytes 196
  18.5 1.0 %copy-start.28 = (f32[16]{0:T(128)S(1)}, f32[16]{0:T(128)}, u32[]{:S(2)}) copy-start(f32[16]{0:T(128)} %get-tuple-element.83) | copy-start | bytes 196
  18.5 1.0 %copy-start.29 = (f32[16]{0:T(128)S(1)}, f32[16]{0:T(128)}, u32[]{:S(2)}) copy-start(f32[16]{0:T(128)} %get-tuple-element.84) | copy-start | bytes 196
  18.5 1.0 %copy-start.30 = (f32[16]{0:T(128)S(1)}, f32[16]{0:T(128)}, u32[]{:S(2)}) copy-start(f32[16]{0:T(128)} %get-tuple-element.85) | copy-start | bytes 196
  18.5 1.0 %copy-start.31 = (f32[16]{0:T(128)S(1)}, f32[16]{0:T(128)}, u32[]{:S(2)}) copy-start(f32[16]{0:T(128)} %get-tuple-element.86) | copy-start | bytes 196
  18.5 1.0 %copy-start.32 = (f32[16]{0:T(128)S(1)}, f32[16]{0:T(128)}, u32[]{:S(2)}) copy-start(f32[16]{0:T(128)} %get-tuple-element.87) | copy-start | bytes 196
  18.5 1.0 %copy-start.33 = (f32[16]{0:T(128)S(1)}, f32[16]{0:T(128)}, u32[]{:S(2)}) copy-start(f32[16]{0:T(128)} %get-tuple-element.88) | copy-start | bytes 196
  18.5 1.0 %copy-start.34 = (f32[16]{0:T(128)S(1)}, f32[16]{0:T(128)}, u32[]{:S(2)}) copy-start(f32[16]{0:T(128)} %get-tuple-element.89) | copy-start | bytes 196
  18.6 1.0 %copy-start.35 = (f32[16]{0:T(128)S(1)}, f32[16]{0:T(128)}, u32[]{:S(2)}) copy-start(f32[16]{0:T(128)} %get-tuple-element.90) | copy-start | bytes 196
  18.6 1.0 %copy-start.36 = (f32[16]{0:T(128)S(1)}, f32[16]{0:T(128)}, u32[]{:S(2)}) copy-start(f32[16]{0:T(128)} %get-tuple-element.91) | copy-start | bytes 196
  18.6 1.0 %copy-start.37 = (f32[16]{0:T(128)S(1)}, f32[16]{0:T(128)}, u32[]{:S(2)}) copy-start(f32[16]{0:T(128)} %get-tuple-element.92) | copy-start | bytes 196
  18.6 1.0 %copy-start.38 = (f32[16]{0:T(128)S(1)}, f32[16]{0:T(128)}, u32[]{:S(2)}) copy-start(f32[16]{0:T(128)} %get-tuple-element.93) | copy-start | bytes 196
  18.6 1.0 %copy-start.39 = (f32[16]{0:T(128)S(1)}, f32[16]{0:T(128)}, u32[]{:S(2)}) copy-start(f32[16]{0:T(128)} %get-tuple-element.94) | copy-start | bytes 196
  18.6 1.0 %copy-start.40 = (f32[16]{0:T(128)S(1)}, f32[16]{0:T(128)}, u32[]{:S(2)}) copy-start(f32[16]{0:T(128)} %get-tuple-element.95) | copy-start | bytes 196
  19.6 4.0 %copy-start.1 = (s32[16,32,512]{2,1,0:T(8,128)S(1)}, s32[16,32,512]{2,1,0:T(8,128)}, u32[]{:S(2)}) copy-start(s32[16,32,512]{2,1,0:T(8,128)} %param.9) | copy-start | bytes 3145732
  19.6 4.0 %copy-start.2 = (f32[16]{0:T(128)S(1)}, f32[16]{0:T(128)}, u32[]{:S(2)}) copy-start(f32[16]{0:T(128)} %get-tuple-element.57) | copy-start | bytes 196
  19.6 4.0 %copy-start.3 = (f32[16]{0:T(128)S(1)}, f32[16]{0:T(128)}, u32[]{:S(2)}) copy-start(f32[16]{0:T(128)} %get-tuple-element.58) | copy-start | bytes 196
  19.6 4.0 %copy-start.4 = (f32[16]{0:T(128)S(1)}, f32[16]{0:T(128)}, u32[]{:S(2)}) copy-start(f32[16]{0:T(128)} %get-tuple-element.59) | copy-start | bytes 196
  19.6 4.0 %copy-start.5 = (f32[16]{0:T(128)S(1)}, f32[16]{0:T(128)}, u32[]{:S(2)}) copy-start(f32[16]{0:T(128)} %get-tuple-element.60) | copy-start | bytes 196
  19.6 4.0 %copy-start.6 = (f32[16]{0:T(128)S(1)}, f32[16]{0:T(128)}, u32[]{:S(2)}) copy-start(f32[16]{0:T(128)} %get-tuple-element.61) | copy-start | bytes 196
  19.6 4.0 %copy-start.7 = (f32[16]{0:T(128)S(1)}, f32[16]{0:T(128)}, u32[]{:S(2)}) copy-start(f32[16]{0:T(128)} %get-tuple-element.62) | copy-start | bytes 196
  19.7 4.0 %copy-start.8 = (f32[16]{0:T(128)S(1)}, f32[16]{0:T(128)}, u32[]{:S(2)}) copy-start(f32[16]{0:T(128)} %get-tuple-element.63) | copy-start | bytes 196
  19.7 4.0 %copy-start.9 = (f32[16]{0:T(128)S(1)}, f32[16]{0:T(128)}, u32[]{:S(2)}) copy-start(f32[16]{0:T(128)} %get-tuple-element.64) | copy-start | bytes 196
  19.7 4.0 %copy-start.10 = (f32[16]{0:T(128)S(1)}, f32[16]{0:T(128)}, u32[]{:S(2)}) copy-start(f32[16]{0:T(128)} %get-tuple-element.65) | copy-start | bytes 196
  19.7 4.0 %copy-start.11 = (f32[16]{0:T(128)S(1)}, f32[16]{0:T(128)}, u32[]{:S(2)}) copy-start(f32[16]{0:T(128)} %get-tuple-element.66) | copy-start | bytes 196
  19.7 4.0 %copy-start.12 = (f32[16]{0:T(128)S(1)}, f32[16]{0:T(128)}, u32[]{:S(2)}) copy-start(f32[16]{0:T(128)} %get-tuple-element.67) | copy-start | bytes 196
  19.7 4.0 %copy-start.13 = (f32[16]{0:T(128)S(1)}, f32[16]{0:T(128)}, u32[]{:S(2)}) copy-start(f32[16]{0:T(128)} %get-tuple-element.68) | copy-start | bytes 196
  19.7 4.0 %copy-start.14 = (f32[16]{0:T(128)S(1)}, f32[16]{0:T(128)}, u32[]{:S(2)}) copy-start(f32[16]{0:T(128)} %get-tuple-element.69) | copy-start | bytes 196
  19.7 4.0 %copy-start.15 = (f32[16]{0:T(128)S(1)}, f32[16]{0:T(128)}, u32[]{:S(2)}) copy-start(f32[16]{0:T(128)} %get-tuple-element.70) | copy-start | bytes 196
  19.7 4.0 %copy-start.16 = (f32[16]{0:T(128)S(1)}, f32[16]{0:T(128)}, u32[]{:S(2)}) copy-start(f32[16]{0:T(128)} %get-tuple-element.71) | copy-start | bytes 196
  19.7 4.0 %copy-start.17 = (f32[16]{0:T(128)S(1)}, f32[16]{0:T(128)}, u32[]{:S(2)}) copy-start(f32[16]{0:T(128)} %get-tuple-element.72) | copy-start | bytes 196
  19.8 4.0 %copy-start.18 = (f32[16]{0:T(128)S(1)}, f32[16]{0:T(128)}, u32[]{:S(2)}) copy-start(f32[16]{0:T(128)} %get-tuple-element.73) | copy-start | bytes 196
  30.8 31.8 %all-to-all-start = ((f32[16,32,512]{2,0,1:T(8,128)}), f32[16,32,512]{2,0,1:T(8,128)S(1)}, u32[]{:S(2)}, u32[]{:S(2)}) async-start(f32[16,32,512]{2,0,1:T(8,128)} %get-tuple-element.113), calls=%async_computation | async-start | bytes 2097152 | tf_op jit(solution)/shard_map/all_to_all | solution.py:127
  67.0 14.4 %copy-start.43 = (s32[16]{0:T(128)S(1)}, s32[16]{0:T(128)}, u32[]{:S(2)}) copy-start(s32[16]{0:T(128)} %param.12) | copy-start | bytes 196
  67.8 9.1 %all-to-all-start.1 = ((f32[4,8,512]{2,1,0:T(8,128)}), f32[4,8,512]{2,1,0:T(8,128)S(1)}, u32[]{:S(2)}, u32[]{:S(2)}) async-start(f32[4,8,512]{2,1,0:T(8,128)} %tile.2), calls=%async_computation.1 | async-start | bytes 131072 | tf_op jit(solution)/shard_map/all_to_all | solution.py:129
  76.9 4.5 %collective-permute-start.4 = (f32[4,512]{1,0:T(4,128)S(1)}, f32[4,512]{1,0:T(4,128)S(1)}, u32[]{:S(2)}, u32[]{:S(2)}) collective-permute-start(f32[4,512]{1,0:T(4,128)S(1)} %get-tuple-element.136), channel_id=1, source_target_pairs={{2,0},{4,2},{6,4},{3,1},{5,3},{7,5},{10,8},{12,10},{14,12},{11,9},... | collective-permute-start | bytes 24584 | tf_op jit(solution)/shard_map/ppermute | solution.py:22
  78.2 3.8 %collective-permute-start.3 = (f32[4,512]{1,0:T(4,128)S(1)}, f32[4,512]{1,0:T(4,128)S(1)}, u32[]{:S(2)}, u32[]{:S(2)}) collective-permute-start(f32[4,512]{1,0:T(4,128)S(1)} %get-tuple-element.135), channel_id=1, source_target_pairs={{0,2},{2,4},{4,6},{1,3},{3,5},{5,7},{8,10},{10,12},{12,14},{9,11},... | collective-permute-start | bytes 24584 | tf_op jit(solution)/shard_map/ppermute | solution.py:21
  82.1 3.8 %collective-permute-start.5 = (f32[4,40]{0,1:T(8,128)S(1)}, f32[4,40]{0,1:T(8,128)S(1)}, u32[]{:S(2)}, u32[]{:S(2)}) collective-permute-start(f32[4,40]{0,1:T(8,128)S(1)} %fusion.55), channel_id=1, source_target_pairs={{0,1},{1,0},{2,3},{3,2},{4,5},{5,4},{6,7},{7,6},{8,9},{9,8},{10,11... | collective-permute-start | bytes 1928 | tf_op jit(solution)/shard_map/ppermute | solution.py:41
where the time goes:
time: 91.4 us; the launch traced here: 90.9 us
  waiting for transfers between devices  36.9 us (40%)
  starting transfers between devices  21.6 us (24%)
  other arithmetic  18.2 us (20%)
  local copies, waits for them, and re-layouts  11.5 us (13%)
  between operations  1.6 us (2%)
    all_to_all x1, waiting for transfers between devices, body(): lax.all_to_all(flagged, 'exp', split_axis=1, concat_axis=0, tiled=True)  26.2 us
    select_n x1, other arithmetic, body(): flagged = jnp.where(bad_pixels == 1, sentinel, warped)  6.99 us
    ppermute x2, starting transfers between devices, _row_halo(): lax.ppermute(lax.slice_in_dim(block, size - width, None, axis=dim), 'row'...  6.48 us
    all_to_all x1, waiting for transfers between devices, body(): lax.all_to_all(jnp.tile(band, (groups, 1)), 'exp', split_axis=0, concat_a...  5.8 us
    all_to_all x1, starting transfers between devices, body(): lax.all_to_all(flagged, 'exp', split_axis=1, concat_axis=0, tiled=True)  5.4 us
    unnamed x94, local copies, waits for them, and re-layouts  4.46 us
    ppermute x2, waiting for transfers between devices, _col_halo(): arrived = lax.ppermute(packed, 'col', [(0, 1), (1, 0)])  4.23 us
    ppermute x2, starting transfers between devices, _col_halo(): arrived = lax.ppermute(packed, 'col', [(0, 1), (1, 0)])  3.87 us
  transfers between devices with their start and end apart: 8, of which 5 were waited for; matrix products, arithmetic and copies ran while one was open for 7% of the time, Pallas kernels for 0%

commit v1 on v0

--- a/solution.py
+++ b/solution.py
@@ -11,6 +11,36 @@
 sentinel = 1000000.0
 half_sentinel = 500000.0
 pivot_span = 16.0
+
+
+def pack_area(x_in, ndim_at, t0):
+    response = x_in.shape
+    value_now = x_in.reshape(
+        *response[:ndim_at], t0, response[ndim_at] // t0, *response[ndim_at + 1 :]
+    )
+    return jnp.moveaxis(value_now, ndim_at, 0)
+
+
+def region_read(m, on_dim):
+    arr_now = list(m.shape[1:])
+    arr_now[on_dim] *= m.shape[0]
+    return jnp.moveaxis(m, 0, on_dim).reshape(arr_now)
+
+
+def cover_links_in(mine, along_axis, raw, local_x):
+    q_next = lax.axis_size(along_axis)
+    everything = lax.axis_index(along_axis)
+    piece_now, carry_in = (q_next, everything)
+    last = pack_area(mine, raw, piece_now)
+    piece_out = last
+    for src_i in range(1, piece_now):
+        v_next, seen_now = ((carry_in + src_i) % piece_now, (carry_in - src_i) % piece_now)
+        f_now = lax.dynamic_index_in_dim(last, v_next, 0)
+        new = range(piece_now)
+        placed = list(map(lambda u: (u, (u + src_i) % piece_now), new))
+        fresh = lax.ppermute(f_now, along_axis, placed)
+        piece_out = lax.dynamic_update_slice_in_dim(piece_out, fresh, seen_now, axis=0)
+    return region_read(piece_out, local_x)
 
 
 def _row_halo(block, dim, width):
@@ -126,9 +156,7 @@
     flagged = jnp.where(bad_pixels == 1, sentinel, warped)
     band = stack_median(lax.all_to_all(flagged, "exp", split_axis=1, concat_axis=0, tiled=True))
     groups = lax.axis_size("exp")
-    median_sky = lax.all_to_all(
-        jnp.tile(band, (groups, 1)), "exp", split_axis=0, concat_axis=0, tiled=True
-    )
+    median_sky = cover_links_in(jnp.tile(band, (groups, 1)), "exp", 0, 0)
     bordered = extended(median_sky, 0, 1, PSF_RADIUS)
     blur = blur_table()
     taps = 2 * PSF_RADIUS + 1

time: 91.4 us -> 87.1 us (0.953)
  waiting for transfers between devices: 36.9 us -> 33.2 us
  local copies, waits for them, and re-layouts: 11.5 us -> 10.3 us
    all_to_all x1 -> x0, waiting for transfers between devices: 5.8 us -> none  [body(): lax.all_to_all(jnp.tile(band, (groups, 1)), 'exp', split_axis=0, concat_a...]
    ppermute x0 -> x3, starting transfers between devices: none -> 3.85 us  [cover_links_in(): fresh = lax.ppermute(f_now, along_axis, placed)]
    all_to_all x1 -> x0, starting transfers between devices: 3.28 us -> none  [body(): lax.all_to_all(jnp.tile(band, (groups, 1)), 'exp', split_axis=0, concat_a...]
    ppermute x0 -> x3, waiting for transfers between devices: none -> 2.18 us  [cover_links_in(): fresh = lax.ppermute(f_now, along_axis, placed)]
    unnamed x94 -> x95, local copies, waits for them, and re-layouts: 4.46 us -> 3.83 us
  transfers between devices with their start and end apart: 8 -> 10, of which waited for: 5 -> 6; matrix products, arithmetic and copies ran while one was open for 7% -> 7% of each run, Pallas kernels for 0% -> 0%
where the time goes in v1:
time: 87.1 us; the launch traced here: 86.8 us
  waiting for transfers between devices  33.2 us (38%)
  starting transfers between devices  22.2 us (25%)
  other arithmetic  18.2 us (21%)
  local copies, waits for them, and re-layouts  10.3 us (12%)
  between operations  1.7 us (2%)
    all_to_all x1, waiting for transfers between devices, body(): lax.all_to_all(flagged, 'exp', split_axis=1, concat_axis=0, tiled=True)  26.2 us
    select_n x1, other arithmetic, body(): flagged = jnp.where(bad_pixels == 1, sentinel, warped)  6.99 us
    ppermute x2, starting transfers between devices, _row_halo(): lax.ppermute(lax.slice_in_dim(block, size - width, None, axis=dim), 'row'...  6.48 us
    all_to_all x1, starting transfers between devices, body(): lax.all_to_all(flagged, 'exp', split_axis=1, concat_axis=0, tiled=True)  5.4 us
    ppermute x2, waiting for transfers between devices, _col_halo(): arrived = lax.ppermute(packed, 'col', [(0, 1), (1, 0)])  4.23 us
    ppermute x2, starting transfers between devices, _col_halo(): arrived = lax.ppermute(packed, 'col', [(0, 1), (1, 0)])  3.87 us
    add x1, other arithmetic, resample_axis(): total = total + coefficients[:, position, None, None] * window  3.86 us
    ppermute x3, starting transfers between devices, cover_links_in(): fresh = lax.ppermute(f_now, along_axis, placed)  3.85 us
  transfers between devices with their start and end apart: 10, of which 6 were waited for; matrix products, arithmetic and copies ran while one was open for 7% of the time, Pallas kernels for 0%

profile of v1, /device:TPU:0, one launch (start us, length us, event | category | flops | bytes accessed | tf_op | source)
XLA Modules:
  0.0 86.8 jit_solution(13438009576152646613)
XLA Ops:
  0.6 1.3 %fusion.134 = (f32[16,11,512]{2,1,0:T(8,128)S(1)}, f32[16,11,512]{2,1,0:T(8,128)S(1)}) fusion(f32[16,32,512]{2,1,0:T(8,128)} %param.8), kind=kLoop, calls=%fused_computation.318 | loop fusion | bytes 1441792 | tf_op jit(solution)/shard_map/slice | solution.py:52
  2.0 0.2 copy.47
  2.2 3.3 %collective-permute-start = (f32[16,11,512]{2,0,1:T(8,128)S(1)}, f32[16,11,512]{2,0,1:T(8,128)}, u32[]{:S(2)}, u32[]{:S(2)}) collective-permute-start(f32[16,11,512]{2,0,1:T(8,128)S(1)} %copy.47), channel_id=1, source_target_pairs={{0,2},{2,4},{4,6},{1,3},{3,5},{5,7},{8,10},{10,12},{12,14},{9,11},... | collective-permute-start | bytes 1081352 | tf_op jit(solution)/shard_map/ppermute | solution.py:51
  5.5 0.2 copy.48
  5.7 1.3 %collective-permute-start.1 = (f32[16,11,512]{2,0,1:T(8,128)S(1)}, f32[16,11,512]{2,0,1:T(8,128)S(1)}, u32[]{:S(2)}, u32[]{:S(2)}) collective-permute-start(f32[16,11,512]{2,0,1:T(8,128)S(1)} %copy.48), channel_id=1, source_target_pairs={{2,0},{4,2},{6,4},{3,1},{5,3},{7,5},{10,8},{12,10},{14,12},{11,9},... | collective-permute-start | bytes 1081352 | tf_op jit(solution)/shard_map/ppermute | solution.py:52
  7.1 0.1 fusion.108
  7.2 0.2 fusion.67
  7.4 0.2 fusion.66
  7.6 0.1 select_reduce_fusion
  7.7 0.8 slice_reduce_fusion.43
  8.5 1.1 %slice_reduce_fusion.44 = (f32[16]{0:T(128)}, f32[16]{0:T(128)}, f32[16]{0:T(128)}, f32[16]{0:T(128)}, f32[16]{0:T(128)}, /*index=5*/f32[16]{0:T(128)}, f32[16]{...) fusion(f32[16,23]{1,0:T(8,128)S(1)} %select_reduce_fusion), kind=kLoop, calls=%fused_computation.204 | loop fusion | bytes 2432 | tf_op jit(solution)/shard_map/slice | solution.py:119
  9.7 1.1 %slice_reduce_fusion.45 = (f32[16]{0:T(128)S(1)}, f32[16]{0:T(128)S(1)}, f32[16]{0:T(128)}, f32[16]{0:T(128)}, f32[16]{0:T(128)}, /*index=5*/f32[16]{0:T(128)}, ...) fusion(f32[16,23]{1,0:T(8,128)S(1)} %select_reduce_fusion.1), kind=kLoop, calls=%fused_computation.205 | loop fusion | bytes 2432 | tf_op jit(solution)/shard_map/slice | solution.py:119
  10.7 1.0 %constant_dynamic-update-slice_fusion.2 = f32[16,54,512]{2,0,1:T(8,128)S(1)} fusion(f32[16,11,512]{2,0,1:T(8,128)} %collective-permute-done), kind=kLoop, calls=%fused_computation.208 | loop fusion | bytes 720896
  11.8 0.6 constant_dynamic-update-slice_fusion.1
  12.4 0.2 fusion.53
  12.6 0.3 copy.40
  12.9 0.1 reshape.189
  13.0 2.4 %collective-permute-start.2 = (f32[11,864]{1,0:T(8,128)S(1)}, f32[11,864]{1,0:T(8,128)S(1)}, u32[]{:S(2)}, u32[]{:S(2)}) collective-permute-start(f32[11,864]{1,0:T(8,128)S(1)} %reshape.189), channel_id=1, source_target_pairs={{0,1},{1,0},{2,3},{3,2},{4,5},{5,4},{6,7},{7,6},{8,9},{9,8},{10,11... | collective-permute-start | bytes 114056 | tf_op jit(solution)/shard_map/ppermute | solution.py:71
  15.4 0.2 slice_reduce_fusion.21
  15.6 1.9 %collective-permute-done.2 = f32[11,864]{1,0:T(8,128)S(1)} collective-permute-done((f32[11,864]{1,0:T(8,128)S(1)}, f32[11,864]{1,0:T(8,128)S(1)}, u32[]{:S(2)}, u32[]{:S(2)}) %collective-permute-start.2) | collective-permute-done | bytes 38048 | tf_op jit(solution)/shard_map/ppermute | solution.py:71
  17.5 0.1 select_n.131
  17.6 0.3 copy.42
  18.0 0.1 select_n.128
  18.1 0.3 copy.41
  18.6 0.7 pad_maximum_fusion
  19.8 3.9 %fusion = f32[16,32,534]{2,0,1:T(8,128)S(1)} fusion(f32[16,54,534]{2,0,1:T(8,128)S(1)} %pad_maximum_fusion, f32[16]{0:T(128)S(1)} %copy-done.25, f32[16]{0:T(128)S(1)} %copy-done.26, f32[16]{0:T(128)S(1)} %copy-done.27, f32[16]{0:T(128)S(1)} %copy-done.28, f32[16]{0:T(128)S(1)} %copy-done.29, f32[16]{0:T(128)S(1)} %copy-done.30, f32[16]{0:T(128)S(1)} %copy-done.31, ...), kind=kLoop, calls=%fused_computation.8 | loop fusion | flops 12303360 | bytes 26248640 | tf_op jit(solution)/shard_map/add | solution.py:119
  23.8 7.0 %broadcast_select_fusion = (f32[16,32,512]{2,0,1:T(8,128)}, f32[16,32,512]{2,0,1:T(8,128)S(1)}, pred[16,32,512]{2,0,1:T(8,128)(4,1)S(1)}) fusion(f32[16,32,534]{2,0,1:T(8,128)S(1)} %fusion, f32[16]{0:T(128)S(1)} %get-tuple-element.56, f32[16]{0:T(128)S(1)} %copy-done.3, f32[16]{0:T(128)S(1)} %copy-done.4, f32[16]{0:T(128)S(1)} %copy-done.5, ...), kind=kLoop, calls=%fused_computation.119 | loop fusion | flops 12320768 | bytes 27526592 | tf_op jit(solution)/shard_map/jit(_where)/select_n | solution.py:156
  30.8 5.4 %all-to-all-start = ((f32[16,32,512]{2,0,1:T(8,128)}), f32[16,32,512]{2,0,1:T(8,128)S(1)}, u32[]{:S(2)}, u32[]{:S(2)}) async-start(f32[16,32,512]{2,0,1:T(8,128)} %get-tuple-element.113), calls=%async_computation | async-start | bytes 2097152 | tf_op jit(solution)/shard_map/all_to_all | solution.py:157
  36.2 0.1 fusion.72
  36.4 26.2 %all-to-all-done = f32[16,32,512]{2,0,1:T(8,128)S(1)} async-done(((f32[16,32,512]{2,0,1:T(8,128)}), f32[16,32,512]{2,0,1:T(8,128)S(1)}, u32[]{:S(2)}, u32[]{:S(2)}) %all-to-all-start) | async-done | bytes 1048608 | tf_op jit(solution)/shard_map/all_to_all | solution.py:157
  62.6 0.6 copy.43
  63.2 0.1 convert_reduce_fusion.1
  63.4 3.6 %while.13 = (s32[]{:T(128)}, f32[8,512]{1,0:T(8,128)S(1)}, f32[8,512]{1,0:T(8,128)S(1)}, f32[64,8,512]{2,1,0:T(8,128)S(1)}, f32[8,512]{1,0:T(8,128)S(1)}, /*index=5*/s32[]{:T(128)}, s32[]{:T(128)}) while((s32[]{:T(128)}, f32[8,512]{1,0:T(8,128)S(1)}, f32[8,512]{1,0:T(8,128)S(1)}, f32[64,8,512]{2,1,0:T(8,128)S(1)}, ...), condition=%wide.region_7.9_spmd.clone, body=%wide.region_5.8_spmd.clone.sunk | while | flops 1110019 | bytes 1302625 | solution.py:135
  63.4 0.1 convert_reduce_fusion.3
  63.6 0.1 convert_reduce_fusion.3
  63.9 0.1 convert_reduce_fusion.3
  64.1 0.1 convert_reduce_fusion.3
  64.3 0.1 convert_reduce_fusion.3
  64.5 0.1 convert_reduce_fusion.3
  64.8 0.1 convert_reduce_fusion.3
  65.0 0.1 convert_reduce_fusion.3
  65.2 0.1 convert_reduce_fusion.3
  65.4 0.1 convert_reduce_fusion.3
  65.7 0.1 convert_reduce_fusion.3
  65.9 0.1 convert_reduce_fusion.3
  66.1 0.1 convert_reduce_fusion.3
  66.4 0.1 convert_reduce_fusion.3
  66.6 0.1 convert_reduce_fusion.3
  66.8 0.1 convert_reduce_fusion.3
  67.0 0.2 fusion.22
  67.3 1.9 %collective-permute-start.4 = (f32[1,8,512]{2,1,0:T(8,128)S(1)}, f32[1,8,512]{2,1,0:T(8,128)S(1)}, u32[]{:S(2)}, u32[]{:S(2)}) collective-permute-start(f32[1,8,512]{2,1,0:T(8,128)S(1)} %bitcast.85), channel_id=1, source_target_pairs={{0,16},{8,24},{16,0},{24,8},{1,17},{9,25},{17,1},{25,9},{2,18},{10... | collective-permute-start | bytes 49160 | tf_op jit(solution)/shard_map/ppermute | solution.py:41
  69.3 1.9 %collective-permute-start.5 = (f32[1,8,512]{2,1,0:T(8,128)S(1)}, f32[1,8,512]{2,1,0:T(8,128)S(1)}, u32[]{:S(2)}, u32[]{:S(2)}) collective-permute-start(f32[1,8,512]{2,1,0:T(8,128)S(1)} %bitcast.86), channel_id=1, source_target_pairs={{0,24},{8,0},{16,8},{24,16},{1,25},{9,1},{17,9},{25,17},{2,26},{10... | collective-permute-start | bytes 49160 | tf_op jit(solution)/shard_map/ppermute | solution.py:41
  71.1 1.8 %collective-permute-done.3 = f32[1,8,512]{2,1,0:T(8,128)S(1)} collective-permute-done((f32[1,8,512]{2,1,0:T(8,128)S(1)}, f32[1,8,512]{2,1,0:T(8,128)S(1)}, u32[]{:S(2)}, u32[]{:S(2)}) %collective-permute-start.3) | collective-permute-done | bytes 16416 | tf_op jit(solution)/shard_map/ppermute | solution.py:41
  73.0 0.4 collective-permute-done.5
  73.4 1.3 %collective-permute-start.7 = (f32[4,512]{1,0:T(4,128)S(1)}, f32[4,512]{1,0:T(4,128)S(1)}, u32[]{:S(2)}, u32[]{:S(2)}) collective-permute-start(f32[4,512]{1,0:T(4,128)S(1)} %get-tuple-element.136), channel_id=1, source_target_pairs={{2,0},{4,2},{6,4},{3,1},{5,3},{7,5},{10,8},{12,10},{14,12},{11,9},... | collective-permute-start | bytes 24584 | tf_op jit(solution)/shard_map/ppermute | solution.py:52
  74.7 3.2 %collective-permute-start.6 = (f32[4,512]{1,0:T(4,128)S(1)}, f32[4,512]{1,0:T(4,128)S(1)}, u32[]{:S(2)}, u32[]{:S(2)}) collective-permute-start(f32[4,512]{1,0:T(4,128)S(1)} %get-tuple-element.135), channel_id=1, source_target_pairs={{0,2},{2,4},{4,6},{1,3},{3,5},{5,7},{8,10},{10,12},{12,14},{9,11},... | collective-permute-start | bytes 24584 | tf_op jit(solution)/shard_map/ppermute | solution.py:51
  77.9 0.6 collective-permute-done.6
  78.6 1.5 %collective-permute-start.8 = (f32[4,40]{0,1:T(8,128)S(1)}, f32[4,40]{0,1:T(8,128)S(1)}, u32[]{:S(2)}, u32[]{:S(2)}) collective-permute-start(f32[4,40]{0,1:T(8,128)S(1)} %fusion.55), channel_id=1, source_target_pairs={{0,1},{1,0},{2,3},{3,2},{4,5},{5,4},{6,7},{7,6},{8,9},{9,8},{10,11... | collective-permute-start | bytes 1928 | tf_op jit(solution)/shard_map/ppermute | solution.py:71
  80.1 2.3 %collective-permute-done.8 = f32[4,40]{0,1:T(8,128)S(1)} collective-permute-done((f32[4,40]{0,1:T(8,128)S(1)}, f32[4,40]{0,1:T(8,128)S(1)}, u32[]{:S(2)}, u32[]{:S(2)}) %collective-permute-start.8) | collective-permute-done | bytes 672 | tf_op jit(solution)/shard_map/ppermute | solution.py:71
  82.4 0.1 pad_maximum_fusion.1
  82.6 0.6 multiply_add_fusion
  83.2 1.3 %fusion.45 = f32[8,32,512]{2,1,0:T(8,128)S(1)} fusion(f32[8,32,520]{2,1,0:T(8,128)S(1)} %multiply_add_fusion, f32[8]{0:T(128)S(1)} %get-tuple-element.142, f32[8]{0:T(128)S(1)} %get-tuple-element.143, f32[8]{0:T(128)S(1)} %get-tuple-element.144, f32[8]{0:T(128)S(1)} %get-tuple-element.145, f32[8]{0:T(128)S(1)} %get-tuple-element.146, ...), kind=kLoop, calls=%fused_computation.103 | loop fusion | flops 2228224 | bytes 5243168 | tf_op jit(solution)/shard_map/add | solution.py:172
  84.5 0.7 subtract_select_fusion
  85.2 1.6 %copy.44 = f32[16,32,512]{2,1,0:T(8,128)} copy(f32[16,32,512]{2,0,1:T(8,128)S(1)} %subtract_select_fusion) | data formatting | bytes 2097152
  (184 shorter events, 1.3 us)
Async XLA Ops:
  2.0 5.1 %copy-start.42 = (s32[16,2]{0,1:T(2,128)S(1)}, s32[16,2]{0,1:T(2,128)}, u32[]{:S(2)}) copy-start(s32[16,2]{0,1:T(2,128)} %param.11) | copy-start | bytes 388
  2.0 5.1 %copy-start.43 = (s32[16,2]{0,1:T(2,128)S(1)}, s32[16,2]{0,1:T(2,128)}, u32[]{:S(2)}) copy-start(s32[16,2]{0,1:T(2,128)} %param.10) | copy-start | bytes 388
  2.2 9.6 %copy-start = (f32[16,32,512]{2,1,0:T(8,128)S(1)}, f32[16,32,512]{2,1,0:T(8,128)}, u32[]{:S(2)}) copy-start(f32[16,32,512]{2,1,0:T(8,128)} %param.8) | copy-start | bytes 3145732
  2.2 8.5 %collective-permute-start = (f32[16,11,512]{2,0,1:T(8,128)S(1)}, f32[16,11,512]{2,0,1:T(8,128)}, u32[]{:S(2)}, u32[]{:S(2)}) collective-permute-start(f32[16,11,512]{2,0,1:T(8,128)S(1)} %copy.47), channel_id=1, source_target_pairs={{0,2},{2,4},{4,6},{1,3},{3,5},{5,7},{8,10},{10,12},{12,14},{9,11},... | collective-permute-start | bytes 1081352 | tf_op jit(solution)/shard_map/ppermute | solution.py:51
  5.7 6.7 %collective-permute-start.1 = (f32[16,11,512]{2,0,1:T(8,128)S(1)}, f32[16,11,512]{2,0,1:T(8,128)S(1)}, u32[]{:S(2)}, u32[]{:S(2)}) collective-permute-start(f32[16,11,512]{2,0,1:T(8,128)S(1)} %copy.48), channel_id=1, source_target_pairs={{2,0},{4,2},{6,4},{3,1},{5,3},{7,5},{10,8},{12,10},{14,12},{11,9},... | collective-permute-start | bytes 1081352 | tf_op jit(solution)/shard_map/ppermute | solution.py:52
  13.0 4.5 %collective-permute-start.2 = (f32[11,864]{1,0:T(8,128)S(1)}, f32[11,864]{1,0:T(8,128)S(1)}, u32[]{:S(2)}, u32[]{:S(2)}) collective-permute-start(f32[11,864]{1,0:T(8,128)S(1)} %reshape.189), channel_id=1, source_target_pairs={{0,1},{1,0},{2,3},{3,2},{4,5},{5,4},{6,7},{7,6},{8,9},{9,8},{10,11... | collective-permute-start | bytes 114056 | tf_op jit(solution)/shard_map/ppermute | solution.py:71
  18.4 1.0 %copy-start.20 = (f32[16]{0:T(128)S(1)}, f32[16]{0:T(128)}, u32[]{:S(2)}) copy-start(f32[16]{0:T(128)} %get-tuple-element.97) | copy-start | bytes 196
  18.4 1.0 %copy-start.21 = (f32[16]{0:T(128)S(1)}, f32[16]{0:T(128)}, u32[]{:S(2)}) copy-start(f32[16]{0:T(128)} %get-tuple-element.98) | copy-start | bytes 196
  18.4 1.0 %copy-start.22 = (f32[16]{0:T(128)S(1)}, f32[16]{0:T(128)}, u32[]{:S(2)}) copy-start(f32[16]{0:T(128)} %get-tuple-element.99) | copy-start | bytes 196
  18.4 1.0 %copy-start.23 = (f32[16]{0:T(128)S(1)}, f32[16]{0:T(128)}, u32[]{:S(2)}) copy-start(f32[16]{0:T(128)} %get-tuple-element.100) | copy-start | bytes 196
  18.4 1.0 %copy-start.24 = (f32[16]{0:T(128)S(1)}, f32[16]{0:T(128)}, u32[]{:S(2)}) copy-start(f32[16]{0:T(128)} %get-tuple-element.78) | copy-start | bytes 196
  18.4 1.0 %copy-start.25 = (f32[16]{0:T(128)S(1)}, f32[16]{0:T(128)}, u32[]{:S(2)}) copy-start(f32[16]{0:T(128)} %get-tuple-element.79) | copy-start | bytes 196
  18.5 1.0 %copy-start.26 = (f32[16]{0:T(128)S(1)}, f32[16]{0:T(128)}, u32[]{:S(2)}) copy-start(f32[16]{0:T(128)} %get-tuple-element.80) | copy-start | bytes 196
  18.5 1.0 %copy-start.27 = (f32[16]{0:T(128)S(1)}, f32[16]{0:T(128)}, u32[]{:S(2)}) copy-start(f32[16]{0:T(128)} %get-tuple-element.81) | copy-start | bytes 196
  18.5 1.0 %copy-start.28 = (f32[16]{0:T(128)S(1)}, f32[16]{0:T(128)}, u32[]{:S(2)}) copy-start(f32[16]{0:T(128)} %get-tuple-element.82) | copy-start | bytes 196
  18.5 1.0 %copy-start.29 = (f32[16]{0:T(128)S(1)}, f32[16]{0:T(128)}, u32[]{:S(2)}) copy-start(f32[16]{0:T(128)} %get-tuple-element.83) | copy-start | bytes 196
  18.5 1.0 %copy-start.30 = (f32[16]{0:T(128)S(1)}, f32[16]{0:T(128)}, u32[]{:S(2)}) copy-start(f32[16]{0:T(128)} %get-tuple-element.84) | copy-start | bytes 196
  18.5 1.0 %copy-start.31 = (f32[16]{0:T(128)S(1)}, f32[16]{0:T(128)}, u32[]{:S(2)}) copy-start(f32[16]{0:T(128)} %get-tuple-element.85) | copy-start | bytes 196
  18.5 1.0 %copy-start.32 = (f32[16]{0:T(128)S(1)}, f32[16]{0:T(128)}, u32[]{:S(2)}) copy-start(f32[16]{0:T(128)} %get-tuple-element.86) | copy-start | bytes 196
  18.5 1.0 %copy-start.33 = (f32[16]{0:T(128)S(1)}, f32[16]{0:T(128)}, u32[]{:S(2)}) copy-start(f32[16]{0:T(128)} %get-tuple-element.87) | copy-start | bytes 196
  18.5 1.0 %copy-start.34 = (f32[16]{0:T(128)S(1)}, f32[16]{0:T(128)}, u32[]{:S(2)}) copy-start(f32[16]{0:T(128)} %get-tuple-element.88) | copy-start | bytes 196
  18.5 1.0 %copy-start.35 = (f32[16]{0:T(128)S(1)}, f32[16]{0:T(128)}, u32[]{:S(2)}) copy-start(f32[16]{0:T(128)} %get-tuple-element.89) | copy-start | bytes 196
  18.6 1.0 %copy-start.36 = (f32[16]{0:T(128)S(1)}, f32[16]{0:T(128)}, u32[]{:S(2)}) copy-start(f32[16]{0:T(128)} %get-tuple-element.90) | copy-start | bytes 196
  18.6 1.0 %copy-start.37 = (f32[16]{0:T(128)S(1)}, f32[16]{0:T(128)}, u32[]{:S(2)}) copy-start(f32[16]{0:T(128)} %get-tuple-element.91) | copy-start | bytes 196
  18.6 1.0 %copy-start.38 = (f32[16]{0:T(128)S(1)}, f32[16]{0:T(128)}, u32[]{:S(2)}) copy-start(f32[16]{0:T(128)} %get-tuple-element.92) | copy-start | bytes 196
  18.6 1.0 %copy-start.39 = (f32[16]{0:T(128)S(1)}, f32[16]{0:T(128)}, u32[]{:S(2)}) copy-start(f32[16]{0:T(128)} %get-tuple-element.93) | copy-start | bytes 196
  18.6 1.0 %copy-start.40 = (f32[16]{0:T(128)S(1)}, f32[16]{0:T(128)}, u32[]{:S(2)}) copy-start(f32[16]{0:T(128)} %get-tuple-element.94) | copy-start | bytes 196
  18.6 1.0 %copy-start.41 = (f32[16]{0:T(128)S(1)}, f32[16]{0:T(128)}, u32[]{:S(2)}) copy-start(f32[16]{0:T(128)} %get-tuple-element.95) | copy-start | bytes 196
  19.6 4.0 %copy-start.1 = (s32[16,32,512]{2,1,0:T(8,128)S(1)}, s32[16,32,512]{2,1,0:T(8,128)}, u32[]{:S(2)}) copy-start(s32[16,32,512]{2,1,0:T(8,128)} %param.9) | copy-start | bytes 3145732
  19.6 4.0 %copy-start.3 = (f32[16]{0:T(128)S(1)}, f32[16]{0:T(128)}, u32[]{:S(2)}) copy-start(f32[16]{0:T(128)} %get-tuple-element.57) | copy-start | bytes 196
  19.6 4.0 %copy-start.4 = (f32[16]{0:T(128)S(1)}, f32[16]{0:T(128)}, u32[]{:S(2)}) copy-start(f32[16]{0:T(128)} %get-tuple-element.58) | copy-start | bytes 196
  19.6 4.0 %copy-start.5 = (f32[16]{0:T(128)S(1)}, f32[16]{0:T(128)}, u32[]{:S(2)}) copy-start(f32[16]{0:T(128)} %get-tuple-element.59) | copy-start | bytes 196
  19.6 4.0 %copy-start.6 = (f32[16]{0:T(128)S(1)}, f32[16]{0:T(128)}, u32[]{:S(2)}) copy-start(f32[16]{0:T(128)} %get-tuple-element.60) | copy-start | bytes 196
  19.6 4.0 %copy-start.7 = (f32[16]{0:T(128)S(1)}, f32[16]{0:T(128)}, u32[]{:S(2)}) copy-start(f32[16]{0:T(128)} %get-tuple-element.61) | copy-start | bytes 196
  19.6 4.0 %copy-start.8 = (f32[16]{0:T(128)S(1)}, f32[16]{0:T(128)}, u32[]{:S(2)}) copy-start(f32[16]{0:T(128)} %get-tuple-element.62) | copy-start | bytes 196
  19.7 4.0 %copy-start.9 = (f32[16]{0:T(128)S(1)}, f32[16]{0:T(128)}, u32[]{:S(2)}) copy-start(f32[16]{0:T(128)} %get-tuple-element.63) | copy-start | bytes 196
  19.7 4.0 %copy-start.10 = (f32[16]{0:T(128)S(1)}, f32[16]{0:T(128)}, u32[]{:S(2)}) copy-start(f32[16]{0:T(128)} %get-tuple-element.64) | copy-start | bytes 196
  19.7 4.0 %copy-start.11 = (f32[16]{0:T(128)S(1)}, f32[16]{0:T(128)}, u32[]{:S(2)}) copy-start(f32[16]{0:T(128)} %get-tuple-element.65) | copy-start | bytes 196
  19.7 4.0 %copy-start.12 = (f32[16]{0:T(128)S(1)}, f32[16]{0:T(128)}, u32[]{:S(2)}) copy-start(f32[16]{0:T(128)} %get-tuple-element.66) | copy-start | bytes 196
  19.7 4.0 %copy-start.13 = (f32[16]{0:T(128)S(1)}, f32[16]{0:T(128)}, u32[]{:S(2)}) copy-start(f32[16]{0:T(128)} %get-tuple-element.67) | copy-start | bytes 196
  19.7 4.0 %copy-start.14 = (f32[16]{0:T(128)S(1)}, f32[16]{0:T(128)}, u32[]{:S(2)}) copy-start(f32[16]{0:T(128)} %get-tuple-element.68) | copy-start | bytes 196
  19.7 4.0 %copy-start.15 = (f32[16]{0:T(128)S(1)}, f32[16]{0:T(128)}, u32[]{:S(2)}) copy-start(f32[16]{0:T(128)} %get-tuple-element.69) | copy-start | bytes 196
  19.7 4.0 %copy-start.16 = (f32[16]{0:T(128)S(1)}, f32[16]{0:T(128)}, u32[]{:S(2)}) copy-start(f32[16]{0:T(128)} %get-tuple-element.70) | copy-start | bytes 196
  19.7 4.0 %copy-start.17 = (f32[16]{0:T(128)S(1)}, f32[16]{0:T(128)}, u32[]{:S(2)}) copy-start(f32[16]{0:T(128)} %get-tuple-element.71) | copy-start | bytes 196
  19.7 4.0 %copy-start.18 = (f32[16]{0:T(128)S(1)}, f32[16]{0:T(128)}, u32[]{:S(2)}) copy-start(f32[16]{0:T(128)} %get-tuple-element.72) | copy-start | bytes 196
  19.8 4.0 %copy-start.19 = (f32[16]{0:T(128)S(1)}, f32[16]{0:T(128)}, u32[]{:S(2)}) copy-start(f32[16]{0:T(128)} %get-tuple-element.73) | copy-start | bytes 196
  30.8 31.8 %all-to-all-start = ((f32[16,32,512]{2,0,1:T(8,128)}), f32[16,32,512]{2,0,1:T(8,128)S(1)}, u32[]{:S(2)}, u32[]{:S(2)}) async-start(f32[16,32,512]{2,0,1:T(8,128)} %get-tuple-element.113), calls=%async_computation | async-start | bytes 2097152 | tf_op jit(solution)/shard_map/all_to_all | solution.py:157
  67.0 10.9 %copy-start.44 = (s32[16]{0:T(128)S(1)}, s32[16]{0:T(128)}, u32[]{:S(2)}) copy-start(s32[16]{0:T(128)} %param.12) | copy-start | bytes 196
  67.2 5.7 %collective-permute-start.3 = (f32[1,8,512]{2,1,0:T(8,128)S(1)}, f32[1,8,512]{2,1,0:T(8,128)S(1)}, u32[]{:S(2)}, u32[]{:S(2)}) collective-permute-start(f32[1,8,512]{2,1,0:T(8,128)S(1)} %bitcast.84), channel_id=1, source_target_pairs={{0,8},{8,16},{16,24},{24,0},{1,9},{9,17},{17,25},{25,1},{2,10},{10... | collective-permute-start | bytes 49160 | tf_op jit(solution)/shard_map/ppermute | solution.py:41
  67.3 5.6 %collective-permute-start.4 = (f32[1,8,512]{2,1,0:T(8,128)S(1)}, f32[1,8,512]{2,1,0:T(8,128)S(1)}, u32[]{:S(2)}, u32[]{:S(2)}) collective-permute-start(f32[1,8,512]{2,1,0:T(8,128)S(1)} %bitcast.85), channel_id=1, source_target_pairs={{0,16},{8,24},{16,0},{24,8},{1,17},{9,25},{17,1},{25,9},{2,18},{10... | collective-permute-start | bytes 49160 | tf_op jit(solution)/shard_map/ppermute | solution.py:41
  69.3 4.1 %collective-permute-start.5 = (f32[1,8,512]{2,1,0:T(8,128)S(1)}, f32[1,8,512]{2,1,0:T(8,128)S(1)}, u32[]{:S(2)}, u32[]{:S(2)}) collective-permute-start(f32[1,8,512]{2,1,0:T(8,128)S(1)} %bitcast.86), channel_id=1, source_target_pairs={{0,24},{8,0},{16,8},{24,16},{1,25},{9,1},{17,9},{25,17},{2,26},{10... | collective-permute-start | bytes 49160 | tf_op jit(solution)/shard_map/ppermute | solution.py:41
  73.3 9.8 %copy-start.2 = (f32[4,8,512]{2,1,0:T(8,128)}, f32[4,8,512]{2,1,0:T(8,128)S(1)}, u32[]{:S(2)}) copy-start(f32[4,8,512]{2,1,0:T(8,128)S(1)} %constant_dynamic-update-slice_fusion.3) | copy-start | bytes 196612
  73.4 4.5 %collective-permute-start.7 = (f32[4,512]{1,0:T(4,128)S(1)}, f32[4,512]{1,0:T(4,128)S(1)}, u32[]{:S(2)}, u32[]{:S(2)}) collective-permute-start(f32[4,512]{1,0:T(4,128)S(1)} %get-tuple-element.136), channel_id=1, source_target_pairs={{2,0},{4,2},{6,4},{3,1},{5,3},{7,5},{10,8},{12,10},{14,12},{11,9},... | collective-permute-start | bytes 24584 | tf_op jit(solution)/shard_map/ppermute | solution.py:52
  74.7 3.8 %collective-permute-start.6 = (f32[4,512]{1,0:T(4,128)S(1)}, f32[4,512]{1,0:T(4,128)S(1)}, u32[]{:S(2)}, u32[]{:S(2)}) collective-permute-start(f32[4,512]{1,0:T(4,128)S(1)} %get-tuple-element.135), channel_id=1, source_target_pairs={{0,2},{2,4},{4,6},{1,3},{3,5},{5,7},{8,10},{10,12},{12,14},{9,11},... | collective-permute-start | bytes 24584 | tf_op jit(solution)/shard_map/ppermute | solution.py:51
  78.6 3.8 %collective-permute-start.8 = (f32[4,40]{0,1:T(8,128)S(1)}, f32[4,40]{0,1:T(8,128)S(1)}, u32[]{:S(2)}, u32[]{:S(2)}) collective-permute-start(f32[4,40]{0,1:T(8,128)S(1)} %fusion.55), channel_id=1, source_target_pairs={{0,1},{1,0},{2,3},{3,2},{4,5},{5,4},{6,7},{7,6},{8,9},{9,8},{10,11... | collective-permute-start | bytes 1928 | tf_op jit(solution)/shard_map/ppermute | solution.py:71
